TPU v7x, 256 devices: a whole 4x4x8 slice. The times are simulated.
256 devices in a mesh: wide: 16 (over z, core), narrow: 16 (over y, x).
Axes of the slice: x: 4, y: 4, z: 8, core: 2. Of those that a mesh axis runs over, the one named last changes fastest.
Arguments:
- screens: bfloat16 [4, 4096, 4096], P(None, 'wide'), may hold values from -3 to 3
- offsets: int32 [2, 128, 4], replicated, may hold values from 0 to 2752, as said below
- valid: int32 [2, 80, 80], P(None, 'narrow'), may hold values from 0 to 1, as said below
- recon: bfloat16 [25600, 5120], P('narrow', 'wide'), may hold values from -0.0390625 to 0.0390625
Outputs:
- slopes: float32 [2, 64, 2, 80, 80], P(None, 'wide', None, 'narrow')
- commands: float32 [64, 5120], P('narrow', 'wide')
Inputs may be any that keep to these rules, and one draw needn't show every extreme that they name: For each coordinate and each layer, the offsets of all items lie within 64 of the smallest, and the largest is exactly 64 above the smallest. In the 5 subaperture rows of one index of narrow, each sensor has at most 300 valid subapertures; in every draw one index of narrow holds exactly 300 for each sensor.
All inputs are finite; a program needn't handle non-finite values.
Results may differ from a plain program's by a relative error of at most 0.0043.
Values may be sent and summed in bfloat16 or wider, within the bound.
No kernel may reach another device: no remote copies, remote signals or barrier semaphores. Data moves between devices by JAX's collectives and lax.ppermute only.
A program may use at most 128 MiB of HBM per device.

v0:
```python
import math
import jax
import jax.numpy as jnp
from jax import lax
from jax.sharding import PartitionSpec as P

L = 4
NSUB = 80
SAMP = 16
NPIX = 32
NSENS = 2
SPREAD = 64
FR_DEV = 4
PUP = 1280


def broadcast(block, axis, source):
    block = jnp.where(lax.axis_index(axis) == source, block, jnp.zeros_like(block))
    return lax.psum(block, axis)


def dft_table(samp, npix):
    sample_ids = jnp.arange(samp * samp, dtype=jnp.int32)
    pixel_ids = jnp.arange(npix * npix, dtype=jnp.int32)
    sample_row = sample_ids // samp
    sample_col = sample_ids % samp
    pixel_row = pixel_ids // npix - npix // 2
    pixel_col = pixel_ids % npix - npix // 2
    phase_turns = jnp.mod(
        sample_row[:, None] * pixel_row[None, :] + sample_col[:, None] * pixel_col[None, :], npix
    )
    angles = phase_turns.astype(jnp.float32) * jnp.float32(-2.0 * math.pi / npix)
    cosine = jnp.cos(angles).astype(jnp.bfloat16)
    sine_part = jnp.sin(angles).astype(jnp.bfloat16)
    top_rows = jnp.concatenate([cosine, sine_part], axis=1)
    bottom_rows = jnp.concatenate([-sine_part, cosine], axis=1)
    return jnp.concatenate([top_rows, bottom_rows], axis=0)


def subaperture_fields(pupil_phase, samp):
    sub_rows = pupil_phase.shape[0] // samp
    sub_cols = pupil_phase.shape[1] // samp
    samples = (
        pupil_phase.reshape(sub_rows, samp, sub_cols, samp)
        .transpose(0, 2, 1, 3)
        .reshape(sub_rows * sub_cols, samp * samp)
    )
    return jnp.concatenate([jnp.cos(samples), jnp.sin(samples)], axis=1).astype(jnp.bfloat16)


def centroids(fields, transform, npix):
    spectrum = jnp.dot(fields, transform, preferred_element_type=jnp.float32)
    pixel_count = npix * npix
    real_part = spectrum[:, :pixel_count]
    imag_part = spectrum[:, pixel_count:]
    intensity = real_part * real_part + imag_part * imag_part
    pixel_ids = jnp.arange(pixel_count, dtype=jnp.int32)
    along_x = (pixel_ids % npix - npix // 2).astype(jnp.float32)
    along_y = (pixel_ids // npix - npix // 2).astype(jnp.float32)
    flux_total = jnp.sum(intensity, axis=1)
    centre_x = jnp.sum(intensity * along_x[None, :], axis=1) / flux_total
    centre_y = jnp.sum(intensity * along_y[None, :], axis=1) / flux_total
    return jnp.stack([centre_x, centre_y], axis=1)


def cut_windows(rows_block, row_first, col_first, pixel_rows):

    def cut_one(row_at, col_at):
        return lax.dynamic_slice(rows_block, (row_at, col_at), (pixel_rows, PUP))

    return jax.vmap(cut_one)(row_first, col_first).astype(jnp.float32)


def body(screens, offsets, valid, recon):
    wide_count = lax.axis_size("wide")
    wide_index = lax.axis_index("wide")
    narrow_index = lax.axis_index("narrow")
    band_rows = screens.shape[1]
    sub_rows = valid.shape[1]
    pixel_rows = sub_rows * SAMP
    union_cols = PUP + SPREAD
    local_items = FR_DEV * NSENS
    own_offsets = lax.dynamic_slice_in_dim(offsets, wide_index * local_items, local_items, 1)
    lowest = jnp.min(offsets, axis=1)
    band_blocks = [
        lax.dynamic_slice_in_dim(screens[which_layer], lowest[1, which_layer], union_cols, 1)
        for which_layer in range(L)
    ]
    pupil_phase = jnp.zeros((local_items, pixel_rows, PUP), jnp.float32)
    for which_layer in range(L):
        group_start = lowest[0, which_layer] + pixel_rows * narrow_index
        root_upper = group_start // band_rows
        root_lower = jnp.minimum(root_upper + 1, wide_count - 1)
        upper_rows = broadcast(band_blocks[which_layer], "wide", root_upper)
        lower_rows = broadcast(band_blocks[which_layer], "wide", root_lower)
        joined_rows = jnp.concatenate([upper_rows, lower_rows], axis=0)
        row_first = (
            own_offsets[0, :, which_layer] + pixel_rows * narrow_index - root_upper * band_rows
        )
        col_first = own_offsets[1, :, which_layer] - lowest[1, which_layer]
        pupil_phase = pupil_phase + cut_windows(joined_rows, row_first, col_first, pixel_rows)
    transform = dft_table(SAMP, NPIX)
    frame_phase = pupil_phase.reshape(FR_DEV, NSENS, pixel_rows, PUP)
    valid_flags = valid.reshape(-1)

    def frame_fields(frame_block):
        return jnp.concatenate(
            [subaperture_fields(frame_block[sensor_index], SAMP) for sensor_index in range(NSENS)],
            axis=0,
        )

    def one_frame(frame_block):
        return centroids(frame_fields(frame_block), transform, NPIX) * valid_flags[:, None].astype(
            jnp.float32
        )

    measured = lax.map(one_frame, frame_phase)
    measured = measured.reshape(FR_DEV, NSENS, sub_rows, NSUB, 2)
    slopes = measured.transpose(4, 0, 1, 2, 3)
    slope_vector = (
        measured.transpose(0, 2, 1, 3, 4)
        .reshape(FR_DEV, sub_rows * NSENS * NSUB * 2)
        .astype(jnp.bfloat16)
    )
    partial_commands = jnp.dot(
        lax.all_gather(slope_vector, "wide", axis=0, tiled=True),
        recon,
        preferred_element_type=jnp.float32,
    )
    commands = lax.psum_scatter(partial_commands, "narrow", scatter_dimension=0, tiled=True)
    return (slopes, commands)


def solution(mesh):
    return jax.shard_map(
        body,
        mesh=mesh,
        in_specs=(P(None, "wide", None), P(), P(None, "narrow", None), P("narrow", "wide")),
        out_specs=(P(None, "wide", None, "narrow", None), P("narrow", "wide")),
        check_vma=False,
    )
```

profile of v0, /device:TPU:32, one launch (start us, length us, event | category | flops | bytes accessed | tf_op | source)
XLA Modules:
  0.0 496.8 jit_solution(6549098456706438841)
XLA Ops:
  16.5 5.7 %fusion.54 = (bf16[1,256,4096]{2,1,0:T(8,128)(2,1)}, bf16[1,256,4096]{2,1,0:T(8,128)(2,1)}, bf16[1,256,4096]{2,1,0:T(8,128)(2,1)S(1)}, bf16[1,256,4096]{2,1,0:T(8,128)(2,1)}) fusion(bf16[4,256,4096]{2,1,0:T(8,128)(2,1)} %param.6), kind=kLoop, calls=%fused_computation.126 | loop fusion | bytes 16777216 | tf_op jit(solution)/shard_map/slice | solution.py:86
  24.7 4.1 select_bitcast_fusion.5
  28.8 3.9 select_bitcast_fusion.1
  33.4 2.6 compare_select_fusion.7
  36.1 4.3 fusion.48
  40.4 4.6 sine_convert_fusion.2
  46.6 113.5 %all-reduce.7.cloned.1.call-done = (bf16[256,1344]{1,0:T(8,128)(2,1)}, bf16[256,1344]{1,0:T(8,128)(2,1)}, bf16[256,1344]{1,0:T(8,128)(2,1)}, bf16[256,1344]{1,0:...) async-done(((bf16[256,1344]{1,0:T(8,128)(2,1)}, bf16[256,1344]{1,0:T(8,128)(2,1)}, ...) | async-done | bytes 5505040 | tf_op jit(solution)/shard_map/psum | solution.py:19
  160.1 2.6 pad_maximum_fusion
  162.9 24.3 %while.18 = (s32[]{:T(128)}, bf16[512,1344]{1,0:T(8,128)(2,1)}, s32[8,2]{0,1:T(2,128)S(1)}, bf16[8,80,1280]{2,1,0:T(8,128)(2,1)S(1)}, s32[]{:T(128)}) while((s32[]{:T(128)}, bf16[512,1344]{1,0:T(8,128)(2,1)}, s32[8,2]{0,1:T(2,128)S(1)}, bf16[8,80,1280]{2,1,0:T(8,128)(2,1)S(1)}, s32[]{:T(128)}) %tuple.146), condition=%wide.while_cond, body=%wide.while_body.sunk | while | flops 2 | bytes 409709 | solution.py:69
  163.5 2.4 bitcast_dynamic-update-slice_fusion.8
  166.6 2.4 bitcast_dynamic-update-slice_fusion.8
  169.6 2.4 bitcast_dynamic-update-slice_fusion.8
  172.7 2.4 bitcast_dynamic-update-slice_fusion.8
  175.7 2.4 bitcast_dynamic-update-slice_fusion.8
  178.8 2.4 bitcast_dynamic-update-slice_fusion.8
  181.8 2.4 bitcast_dynamic-update-slice_fusion.8
  184.9 2.4 bitcast_dynamic-update-slice_fusion.8
  187.2 2.9 pad_maximum_fusion.1
  191.5 28.6 %while.19 = (s32[]{:T(128)}, bf16[512,1344]{1,0:T(8,128)(2,1)}, s32[8,2]{0,1:T(2,128)S(1)}, bf16[8,80,1280]{2,1,0:T(8,128)(2,1)}, s32[]{:T(128)}) while((s32[]{:T(128)}, bf16[512,1344]{1,0:T(8,128)(2,1)}, s32[8,2]{0,1:T(2,128)S(1)}, bf16[8,80,1280]{2,1,0:T(8,128)(2,1)}, s32[]{:T(128)}) %tuple.143), condition=%wide.while_cond.1, body=%wide.while_body.1.sunk | while | flops 2 | bytes 411233 | solution.py:69
  192.1 3.0 bitcast_dynamic-update-slice_fusion.9
  195.7 3.0 bitcast_dynamic-update-slice_fusion.9
  199.3 3.0 bitcast_dynamic-update-slice_fusion.9
  202.8 3.0 bitcast_dynamic-update-slice_fusion.9
  206.4 3.0 bitcast_dynamic-update-slice_fusion.9
  210.0 3.0 bitcast_dynamic-update-slice_fusion.9
  213.5 3.0 bitcast_dynamic-update-slice_fusion.9
  217.2 3.0 bitcast_dynamic-update-slice_fusion.9
  220.1 2.4 pad_maximum_fusion.2
  222.6 23.4 %while.20 = (s32[]{:T(128)}, bf16[512,1344]{1,0:T(8,128)(2,1)}, s32[8,2]{0,1:T(2,128)S(1)}, bf16[8,80,1280]{2,1,0:T(8,128)(2,1)S(1)}, s32[]{:T(128)}) while((s32[]{:T(128)}, bf16[512,1344]{1,0:T(8,128)(2,1)}, s32[8,2]{0,1:T(2,128)S(1)}, bf16[8,80,1280]{2,1,0:T(8,128)(2,1)S(1)}, s32[]{:T(128)}) %tuple.140), condition=%wide.while_cond.2, body=%wide.while_body.2.sunk | while | flops 2 | bytes 409709 | solution.py:69
  223.3 2.3 bitcast_dynamic-update-slice_fusion.10
  226.2 2.3 bitcast_dynamic-update-slice_fusion.10
  229.1 2.3 bitcast_dynamic-update-slice_fusion.10
  232.1 2.3 bitcast_dynamic-update-slice_fusion.10
  235.0 2.3 bitcast_dynamic-update-slice_fusion.10
  237.9 2.3 bitcast_dynamic-update-slice_fusion.10
  240.8 2.3 bitcast_dynamic-update-slice_fusion.10
  243.8 2.3 bitcast_dynamic-update-slice_fusion.10
  246.1 2.9 pad_maximum_fusion.3
  249.0 24.1 %while.21 = (s32[]{:T(128)}, bf16[512,1344]{1,0:T(8,128)(2,1)}, s32[8,2]{0,1:T(2,128)S(1)}, bf16[8,80,1280]{2,1,0:T(8,128)(2,1)S(1)}, s32[]{:T(128)}) while((s32[]{:T(128)}, bf16[512,1344]{1,0:T(8,128)(2,1)}, s32[8,2]{0,1:T(2,128)S(1)}, bf16[8,80,1280]{2,1,0:T(8,128)(2,1)S(1)}, s32[]{:T(128)}) %tuple.137), condition=%wide.while_cond.3, body=%wide.while_body.3.sunk | while | flops 2 | bytes 409709 | solution.py:69
  249.7 2.3 bitcast_dynamic-update-slice_fusion.11
  252.7 2.3 bitcast_dynamic-update-slice_fusion.11
  255.7 2.3 bitcast_dynamic-update-slice_fusion.11
  258.8 2.3 bitcast_dynamic-update-slice_fusion.11
  261.8 2.3 bitcast_dynamic-update-slice_fusion.11
  264.8 2.3 bitcast_dynamic-update-slice_fusion.11
  267.8 2.3 bitcast_dynamic-update-slice_fusion.11
  270.8 2.3 bitcast_dynamic-update-slice_fusion.11
  273.2 4.9 convert_add_fusion
  278.1 98.5 %while.17 = (s32[]{:T(128)}, f32[4,800,2]{1,2,0:T(2,128)S(1)}, f32[4,2,80,1280]{3,2,1,0:T(8,128)}, bf16[512,2048]{1,0:T(8,128)(2,1)}, f32[800,1]{0,1:T(1,128)S(1)}, /*index=5*/s32[]{:T(128)}, s32[]{:T(128)}, s32[]{}, f32[]{:T(128)}) while((s32[]{:T(128)}, f32[4,800,2]{1,2,0:T(2,128)S(1)}, f32[4,2,80,1280]{3,2,1,0:T(8,128)}, ...), condition=%wide.region_13.14_spmd, body=%wide.region_9.13_spmd.sunk | while | flops 1687980416 | bytes 22656888 | solution.py:117
  278.1 5.2 %cosine_convert_fusion.4 = (bf16[1,1,80,1280]{3,2,1,0:T(8,128)(2,1)}, bf16[1,1,80,1280]{3,2,1,0:T(8,128)(2,1)}, bf16[1,1,80,1280]{3,2,1,0:T(8,128)(2,1)S(1)}, bf16[1,1,80,1280]{3,2,1,0:T(8,128)(2,1)S(1)}) fusion(f32[4,2,80,1280]{3,2,1,0:T(8,128)} %get-tuple-element.498, s32[]{:T(128)} %get-tuple-element.487, s32[]{:T(128)S(6)} %add.480), kind=kLoop, calls=%fused_computation.24.clone.1 | loop fusion | flops 409600 | bytes 1638408 | tf_op jit(solution)/shard_map/convert.15
  286.5 2.2 cos.49
  290.8 2.2 sin.47
  297.6 3.9 fusion.73
  302.7 5.2 %cosine_convert_fusion.4 = (bf16[1,1,80,1280]{3,2,1,0:T(8,128)(2,1)}, bf16[1,1,80,1280]{3,2,1,0:T(8,128)(2,1)}, bf16[1,1,80,1280]{3,2,1,0:T(8,128)(2,1)S(1)}, bf16[1,1,80,1280]{3,2,1,0:T(8,128)(2,1)S(1)}) fusion(f32[4,2,80,1280]{3,2,1,0:T(8,128)} %get-tuple-element.498, s32[]{:T(128)} %get-tuple-element.487, s32[]{:T(128)S(6)} %add.480), kind=kLoop, calls=%fused_computation.24.clone.1 | loop fusion | flops 409600 | bytes 1638408 | tf_op jit(solution)/shard_map/convert.15
  311.2 2.2 cos.49
  322.2 3.8 fusion.73
  327.3 5.2 %cosine_convert_fusion.4 = (bf16[1,1,80,1280]{3,2,1,0:T(8,128)(2,1)}, bf16[1,1,80,1280]{3,2,1,0:T(8,128)(2,1)}, bf16[1,1,80,1280]{3,2,1,0:T(8,128)(2,1)S(1)}, bf16[1,1,80,1280]{3,2,1,0:T(8,128)(2,1)S(1)}) fusion(f32[4,2,80,1280]{3,2,1,0:T(8,128)} %get-tuple-element.498, s32[]{:T(128)} %get-tuple-element.487, s32[]{:T(128)S(6)} %add.480), kind=kLoop, calls=%fused_computation.24.clone.1 | loop fusion | flops 409600 | bytes 1638408 | tf_op jit(solution)/shard_map/convert.15
  335.8 2.2 cos.49
  340.0 2.2 sin.47
  346.8 3.9 fusion.73
  351.9 5.2 %cosine_convert_fusion.4 = (bf16[1,1,80,1280]{3,2,1,0:T(8,128)(2,1)}, bf16[1,1,80,1280]{3,2,1,0:T(8,128)(2,1)}, bf16[1,1,80,1280]{3,2,1,0:T(8,128)(2,1)S(1)}, bf16[1,1,80,1280]{3,2,1,0:T(8,128)(2,1)S(1)}) fusion(f32[4,2,80,1280]{3,2,1,0:T(8,128)} %get-tuple-element.498, s32[]{:T(128)} %get-tuple-element.487, s32[]{:T(128)S(6)} %add.480), kind=kLoop, calls=%fused_computation.24.clone.1 | loop fusion | flops 409600 | bytes 1638408 | tf_op jit(solution)/shard_map/convert.15
  371.5 3.9 fusion.73
  377.3 18.1 %all-gather = bf16[16,4,1600]{2,1,0:T(4,128)(2,1)S(1)} all-gather(bf16[1,4,1600]{2,1,0:T(4,128)(2,1)S(1)} %copy.28), channel_id=1, replica_groups=mesh['wide'=16,'narrow'=16] {'wide'}, dimensions={0}, use_global_device_ids=true | all-gather | bytes 217600 | tf_op jit(solution)/shard_map/all_gather | solution.py:126
  398.5 90.2 %all-reduce.5.cloned.1.call-done = f32[64,320]{1,0:T(8,128)} async-done(((f32[64,320]{1,0:T(8,128)}), f32[64,320]{1,0:T(8,128)}) %all-reduce.5.cloned.1.call-update) | async-done | bytes 81936
  (181 shorter events, 81.5 us)
Async XLA Ops:
  7.2 388.3 %copy-start = (bf16[1600,320]{0,1:T(8,128)(2,1)S(1)}, bf16[1600,320]{0,1:T(8,128)(2,1)}, u32[]{:S(2)}) copy-start(bf16[1600,320]{0,1:T(8,128)(2,1)} %param.9) | copy-start | bytes 3072004
  7.2 152.9 %all-reduce.7.cloned.1.call-start = ((), (), s32[]{:S(2)}) async-start(), calls=%async_computation.1 | async-start | bytes 11534336 | tf_op jit(solution)/shard_map/psum | solution.py:19
  32.6 0.7 copy-start.7
  32.6 0.8 copy-start.6
  32.7 456.0 %all-reduce.5.cloned.1.call-start = ((), (), s32[]{:S(2)}) async-start(), calls=%async_computation | async-start | bytes 196608
  162.7 24.5 %copy-start.5 = (bf16[256,1344]{1,0:T(8,128)(2,1)S(1)}, bf16[256,1344]{1,0:T(8,128)(2,1)}, u32[]{:S(2)}) copy-start(bf16[256,1344]{1,0:T(8,128)(2,1)} %get-tuple-element.187) | copy-start | bytes 2064388
  187.2 4.3 copy-start.1
  190.2 29.9 %copy-start.4 = (bf16[256,1344]{1,0:T(8,128)(2,1)S(1)}, bf16[256,1344]{1,0:T(8,128)(2,1)}, u32[]{:S(2)}) copy-start(bf16[256,1344]{1,0:T(8,128)(2,1)} %get-tuple-element.185) | copy-start | bytes 2064388
  222.5 23.5 %copy-start.3 = (bf16[256,1344]{1,0:T(8,128)(2,1)S(1)}, bf16[256,1344]{1,0:T(8,128)(2,1)}, u32[]{:S(2)}) copy-start(bf16[256,1344]{1,0:T(8,128)(2,1)} %get-tuple-element.183) | copy-start | bytes 2064388
  246.0 2.9 copy-start.2
  376.5 20.1 %copy-start.8 = (u32[256]{0:T(256)S(1)}, u32[256]{0:T(256)}, u32[]{:S(2)}) copy-start(u32[256]{0:T(256)} %constant.269) | copy-start | bytes 3076
Sparse Core Ops, SparseCore 0:
  32.8 127.2 all-reduce.6
  396.7 91.9 all-reduce.4
where the time goes:
time: 500 us; the launch traced here: 497 us
  waiting for transfers between devices  204 us (41%)
  local copies, waits for them, and re-layouts  169 us (34%)
  other arithmetic  63.1 us (13%)
  between operations  25.2 us (5%)
  blocking collectives  18.1 us (4%)
  matrix products  16.5 us (3%)
    psum x1, waiting for transfers between devices, broadcast(): return lax.psum(block, axis)  114 us
    gather x96, local copies, waits for them, and re-layouts  100 us
    unnamed x3, waiting for transfers between devices  90.2 us
    cos x24, local copies, waits for them, and re-layouts, subaperture_fields(): jnp.cos(samples)  29.9 us
    sin x24, local copies, waits for them, and re-layouts, subaperture_fields(): jnp.sin(samples)  27.2 us
    another operation x8, other arithmetic  20.9 us
    all_gather x1, blocking collectives, body(): lax.all_gather(slope_vector, 'wide', axis=0, tiled=True)  18.1 us
    dot_general x4, matrix products, centroids(): spectrum = jnp.dot(fields, transform, preferred_element_type=jnp.float32)  15.4 us
  transfers between devices with their start and end apart: 2, of which 2 were waited for; matrix products, arithmetic and copies ran while one was open for 3% of the time, Pallas kernels for 0%

commit v1 on v0

--- a/solution.py
+++ b/solution.py
@@ -16,7 +16,7 @@
 
 def broadcast(block, axis, source):
     block = jnp.where(lax.axis_index(axis) == source, block, jnp.zeros_like(block))
-    return lax.psum(block, axis)
+    return jnp.sum(lax.all_gather(block, axis), axis=0)
 
 
 def dft_table(samp, npix):

time: 500 us -> 862 us (1.72)
  waiting for transfers between devices: 204 us -> 493 us
  other arithmetic: 63.1 us -> 107 us
  local copies, waits for them, and re-layouts: 169 us -> 194 us
    all_gather x0 -> x8, waiting for transfers between devices: none -> 400 us  [broadcast(): return jnp.sum(lax.all_gather(block, axis), axis=0)]
    psum x1 -> x0, waiting for transfers between devices: 114 us -> none  [broadcast(): return lax.psum(block, axis)]
    reduce_sum x0 -> x8, other arithmetic: none -> 51.1 us  [broadcast(): return jnp.sum(lax.all_gather(block, axis), axis=0)]
    unnamed x27 -> x29, local copies, waits for them, and re-layouts: 5.09 us -> 18.2 us
    unnamed x3 -> x10, waiting for transfers between devices: 90.2 us -> 93.7 us
  transfers between devices with their start and end apart: 2 -> 9, of which waited for: 2 -> 8; matrix products, arithmetic and copies ran while one was open for 3% -> 19% of each run, Pallas kernels for 0% -> 0%
where the time goes in v1:
time: 862 us; the launch traced here: 855 us
  waiting for transfers between devices  493 us (57%)
  local copies, waits for them, and re-layouts  194 us (23%)
  other arithmetic  107 us (12%)
  between operations  25.4 us (3%)
  blocking collectives  17.1 us (2%)
  matrix products  16.5 us (2%)
    all_gather x8, waiting for transfers between devices, broadcast(): return jnp.sum(lax.all_gather(block, axis), axis=0)  400 us
    gather x96, local copies, waits for them, and re-layouts  105 us
    unnamed x10, waiting for transfers between devices  93.7 us
    reduce_sum x8, other arithmetic, broadcast(): return jnp.sum(lax.all_gather(block, axis), axis=0)  51.1 us
    cos x24, local copies, waits for them, and re-layouts, subaperture_fields(): jnp.cos(samples)  30 us
    sin x24, local copies, waits for them, and re-layouts, subaperture_fields(): jnp.sin(samples)  27 us
    another operation x8, other arithmetic  20.9 us
    unnamed x29, local copies, waits for them, and re-layouts  18.2 us
  transfers between devices with their start and end apart: 9, of which 8 were waited for; matrix products, arithmetic and copies ran while one was open for 19% of the time, Pallas kernels for 0%

profile of v1, /device:TPU:32, one launch (start us, length us, event | category | flops | bytes accessed | tf_op | source)
XLA Modules:
  0.0 854.8 jit_solution(10217909437146179752)
XLA Ops:
  12.1 5.7 fusion.54
  19.0 3.4 constant_dynamic-slice_fusion.11
  24.6 2.3 broadcast_select_fusion.7
  30.7 2.3 broadcast_select_fusion.5
  38.1 3.2 constant_dynamic-slice_fusion.9
  48.1 2.6 compare_select_fusion.7
  50.8 4.3 fusion.48
  55.1 4.6 sine_convert_fusion.2
  61.2 34.9 %all-gather.10.cloned.1.call-done = bf16[16,256,1344]{1,2,0:T(8,128)(2,1)} async-done(((bf16[1,256,1344]{1,2,0:T(8,128)(2,1)}), bf16[16,256,1344]{1,2,0:T(8,128)(2,1)}) %all-gather.10.cloned.1.call-update) | async-done | bytes 11010064 | tf_op jit(solution)/shard_map/all_gather | solution.py:19
  96.1 6.1 reduce_sum.135
  102.2 62.6 %all-gather.12.cloned.1.call-done = bf16[16,256,1344]{1,2,0:T(8,128)(2,1)} async-done(((bf16[1,256,1344]{1,2,0:T(8,128)(2,1)}), bf16[16,256,1344]{1,2,0:T(8,128)(2,1)}) %all-gather.12.cloned.1.call-update) | async-done | bytes 11010064 | tf_op jit(solution)/shard_map/all_gather | solution.py:19
  164.8 6.7 reduce_sum.136
  174.3 59.2 %all-gather.14.cloned.1.call-done = bf16[16,256,1344]{1,2,0:T(8,128)(2,1)} async-done(((bf16[1,256,1344]{1,2,0:T(8,128)(2,1)}), bf16[16,256,1344]{1,2,0:T(8,128)(2,1)}) %all-gather.14.cloned.1.call-update) | async-done | bytes 11010064 | tf_op jit(solution)/shard_map/all_gather | solution.py:19
  233.5 6.1 reduce_sum.137
  239.5 62.4 %all-gather.16.cloned.1.call-done = bf16[16,256,1344]{1,2,0:T(8,128)(2,1)} async-done(((bf16[1,256,1344]{1,2,0:T(8,128)(2,1)}), bf16[16,256,1344]{1,2,0:T(8,128)(2,1)}) %all-gather.16.cloned.1.call-update) | async-done | bytes 11010064 | tf_op jit(solution)/shard_map/all_gather | solution.py:19
  302.0 6.7 reduce_sum.138
  311.6 58.9 %all-gather.18.cloned.1.call-done = bf16[16,256,1344]{1,2,0:T(8,128)(2,1)} async-done(((bf16[1,256,1344]{1,2,0:T(8,128)(2,1)}), bf16[16,256,1344]{1,2,0:T(8,128)(2,1)}) %all-gather.18.cloned.1.call-update) | async-done | bytes 11010064 | tf_op jit(solution)/shard_map/all_gather | solution.py:19
  370.5 6.1 reduce_sum.139
  376.6 62.4 %all-gather.20.cloned.1.call-done = bf16[16,256,1344]{1,2,0:T(8,128)(2,1)} async-done(((bf16[1,256,1344]{1,2,0:T(8,128)(2,1)}), bf16[16,256,1344]{1,2,0:T(8,128)(2,1)}) %all-gather.20.cloned.1.call-update) | async-done | bytes 11010064 | tf_op jit(solution)/shard_map/all_gather | solution.py:19
  439.0 6.7 reduce_sum.140
  448.5 59.2 %all-gather.22.cloned.1.call-done = bf16[16,256,1344]{1,2,0:T(8,128)(2,1)} async-done(((bf16[1,256,1344]{1,2,0:T(8,128)(2,1)}), bf16[16,256,1344]{1,2,0:T(8,128)(2,1)}) %all-gather.22.cloned.1.call-update) | async-done | bytes 11010064 | tf_op jit(solution)/shard_map/all_gather | solution.py:19
  507.7 6.1 reduce_sum.141
  513.8 23.0 %while.18 = (s32[]{:T(128)}, bf16[512,1344]{1,0:T(8,128)(2,1)}, s32[8,2]{0,1:T(2,128)S(1)}, bf16[8,80,1280]{2,1,0:T(8,128)(2,1)S(1)}, s32[]{:T(128)}) while((s32[]{:T(128)}, bf16[512,1344]{1,0:T(8,128)(2,1)}, s32[8,2]{0,1:T(2,128)S(1)}, bf16[8,80,1280]{2,1,0:T(8,128)(2,1)S(1)}, s32[]{:T(128)}) %tuple.149), condition=%wide.while_cond, body=%wide.while_body.sunk | while | flops 2 | bytes 409709 | solution.py:69
  531.7 2.3 bitcast_dynamic-update-slice_fusion.8
  538.2 29.9 %while.19 = (s32[]{:T(128)}, bf16[512,1344]{1,0:T(8,128)(2,1)}, s32[8,2]{0,1:T(2,128)S(1)}, bf16[8,80,1280]{2,1,0:T(8,128)(2,1)}, s32[]{:T(128)}) while((s32[]{:T(128)}, bf16[512,1344]{1,0:T(8,128)(2,1)}, s32[8,2]{0,1:T(2,128)S(1)}, bf16[8,80,1280]{2,1,0:T(8,128)(2,1)}, s32[]{:T(128)}) %tuple.146), condition=%wide.while_cond.1, body=%wide.while_body.1.sunk | while | flops 2 | bytes 411233 | solution.py:69
  538.9 3.1 bitcast_dynamic-update-slice_fusion.9
  542.6 3.1 bitcast_dynamic-update-slice_fusion.9
  546.4 3.1 bitcast_dynamic-update-slice_fusion.9
  550.1 3.1 bitcast_dynamic-update-slice_fusion.9
  553.8 3.1 bitcast_dynamic-update-slice_fusion.9
  557.6 3.1 bitcast_dynamic-update-slice_fusion.9
  561.3 3.1 bitcast_dynamic-update-slice_fusion.9
  565.0 3.1 bitcast_dynamic-update-slice_fusion.9
  569.4 29.0 %while.20 = (s32[]{:T(128)}, bf16[512,1344]{1,0:T(8,128)(2,1)}, s32[8,2]{0,1:T(2,128)S(1)}, bf16[8,80,1280]{2,1,0:T(8,128)(2,1)}, s32[]{:T(128)}) while((s32[]{:T(128)}, bf16[512,1344]{1,0:T(8,128)(2,1)}, s32[8,2]{0,1:T(2,128)S(1)}, bf16[8,80,1280]{2,1,0:T(8,128)(2,1)}, s32[]{:T(128)}) %tuple.143), condition=%wide.while_cond.2, body=%wide.while_body.2.sunk | while | flops 2 | bytes 411233 | solution.py:69
  570.1 3.0 bitcast_dynamic-update-slice_fusion.10
  573.7 3.0 bitcast_dynamic-update-slice_fusion.10
  577.3 3.0 bitcast_dynamic-update-slice_fusion.10
  580.9 3.0 bitcast_dynamic-update-slice_fusion.10
  584.6 3.0 bitcast_dynamic-update-slice_fusion.10
  588.2 3.0 bitcast_dynamic-update-slice_fusion.10
  591.8 3.0 bitcast_dynamic-update-slice_fusion.10
  595.4 3.0 bitcast_dynamic-update-slice_fusion.10
  598.4 6.7 reduce_sum.142
  608.0 23.3 %while.21 = (s32[]{:T(128)}, bf16[512,1344]{1,0:T(8,128)(2,1)}, s32[8,2]{0,1:T(2,128)S(1)}, bf16[8,80,1280]{2,1,0:T(8,128)(2,1)S(1)}, s32[]{:T(128)}) while((s32[]{:T(128)}, bf16[512,1344]{1,0:T(8,128)(2,1)}, s32[8,2]{0,1:T(2,128)S(1)}, bf16[8,80,1280]{2,1,0:T(8,128)(2,1)S(1)}, s32[]{:T(128)}) %tuple.140), condition=%wide.while_cond.3, body=%wide.while_body.3.sunk | while | flops 2 | bytes 409709 | solution.py:69
  608.6 2.3 bitcast_dynamic-update-slice_fusion.11
  611.5 2.3 bitcast_dynamic-update-slice_fusion.11
  614.4 2.3 bitcast_dynamic-update-slice_fusion.11
  617.4 2.3 bitcast_dynamic-update-slice_fusion.11
  620.3 2.3 bitcast_dynamic-update-slice_fusion.11
  623.2 2.3 bitcast_dynamic-update-slice_fusion.11
  626.1 2.3 bitcast_dynamic-update-slice_fusion.11
  629.0 2.3 bitcast_dynamic-update-slice_fusion.11
  631.3 4.8 convert_add_fusion
  636.1 98.5 %while.17 = (s32[]{:T(128)}, f32[4,800,2]{1,2,0:T(2,128)S(1)}, f32[4,2,80,1280]{3,2,1,0:T(8,128)}, bf16[512,2048]{1,0:T(8,128)(2,1)}, f32[800,1]{0,1:T(1,128)S(1)}, /*index=5*/s32[]{:T(128)}, s32[]{:T(128)}, s32[]{}, f32[]{:T(128)}) while((s32[]{:T(128)}, f32[4,800,2]{1,2,0:T(2,128)S(1)}, f32[4,2,80,1280]{3,2,1,0:T(8,128)}, ...), condition=%wide.region_13.14_spmd, body=%wide.region_9.13_spmd.sunk | while | flops 1687980416 | bytes 22656888 | solution.py:117
  636.3 5.2 cosine_convert_fusion.4
  655.8 3.9 fusion.73
  660.9 5.2 cosine_convert_fusion.4
  680.4 3.9 fusion.73
  685.5 5.2 cosine_convert_fusion.4
  705.0 3.9 fusion.73
  710.1 5.2 cosine_convert_fusion.4
  729.6 3.9 fusion.73
  735.4 17.1 %all-gather = bf16[16,4,1600]{2,1,0:T(4,128)(2,1)S(1)} all-gather(bf16[1,4,1600]{2,1,0:T(4,128)(2,1)S(1)} %copy.48), channel_id=1, replica_groups=mesh['wide'=16,'narrow'=16] {'wide'}, dimensions={0}, use_global_device_ids=true | all-gather | bytes 217600 | tf_op jit(solution)/shard_map/all_gather | solution.py:126
  755.6 91.1 %all-reduce.3.cloned.1.call-done = f32[64,320]{1,0:T(8,128)} async-done(((f32[64,320]{1,0:T(8,128)}), f32[64,320]{1,0:T(8,128)}) %all-reduce.3.cloned.1.call-update) | async-done | bytes 81936
  (216 shorter events, 131.1 us)
Async XLA Ops:
  7.2 745.4 %copy-start = (bf16[1600,320]{0,1:T(8,128)(2,1)S(1)}, bf16[1600,320]{0,1:T(8,128)(2,1)}, u32[]{:S(2)}) copy-start(bf16[1600,320]{0,1:T(8,128)(2,1)} %param.9) | copy-start | bytes 3072004
  7.2 89.0 %all-gather.10.cloned.1.call-start = ((), (), s32[]{:S(2)}) async-start(), calls=%async_computation | async-start | bytes 11698176 | tf_op jit(solution)/shard_map/all_gather | solution.py:19
  27.0 137.8 %all-gather.12.cloned.1.call-start = ((), (), s32[]{:S(2)}) async-start(), calls=%async_computation.1 | async-start | bytes 11698176 | tf_op jit(solution)/shard_map/all_gather | solution.py:19
  27.7 205.7 %all-gather.14.cloned.1.call-start = ((), (), s32[]{:S(2)}) async-start(), calls=%async_computation.2 | async-start | bytes 11698176 | tf_op jit(solution)/shard_map/all_gather | solution.py:19
  33.0 269.0 %all-gather.16.cloned.1.call-start = ((), (), s32[]{:S(2)}) async-start(), calls=%async_computation.3 | async-start | bytes 11698176 | tf_op jit(solution)/shard_map/all_gather | solution.py:19
  33.6 336.9 %all-gather.18.cloned.1.call-start = ((), (), s32[]{:S(2)}) async-start(), calls=%async_computation.4 | async-start | bytes 11698176 | tf_op jit(solution)/shard_map/all_gather | solution.py:19
  42.7 2.5 copy-start.2
  43.8 395.2 %all-gather.20.cloned.1.call-start = ((), (), s32[]{:S(2)}) async-start(), calls=%async_computation.5 | async-start | bytes 11698176 | tf_op jit(solution)/shard_map/all_gather | solution.py:19
  44.4 463.2 %all-gather.22.cloned.1.call-start = ((), (), s32[]{:S(2)}) async-start(), calls=%async_computation.6 | async-start | bytes 11698176 | tf_op jit(solution)/shard_map/all_gather | solution.py:19
  45.4 2.6 copy-start.4
  45.4 2.7 copy-start.3
  46.7 551.7 %all-gather.24.cloned.1.call-start = ((), (), s32[]{:S(2)}) async-start(), calls=%async_computation.7 | async-start | bytes 11698176 | tf_op jit(solution)/shard_map/all_gather | solution.py:19
  47.4 799.3 %all-reduce.3.cloned.1.call-start = ((), (), s32[]{:S(2)}) async-start(), calls=%async_computation.8 | async-start | bytes 196608
  536.8 32.6 %copy-start.1 = (bf16[8,80,1280]{2,1,0:T(8,128)(2,1)}, bf16[8,80,1280]{2,1,0:T(8,128)(2,1)S(1)}, u32[]{:S(2)}) copy-start(bf16[8,80,1280]{2,1,0:T(8,128)(2,1)S(1)} %get-tuple-element.107) | copy-start | bytes 4915204
  734.6 19.0 %copy-start.5 = (u32[256]{0:T(256)S(1)}, u32[256]{0:T(256)}, u32[]{:S(2)}) copy-start(u32[256]{0:T(256)} %constant.278) | copy-start | bytes 3076
Sparse Core Ops, SparseCore 0:
  27.1 68.9 all-gather.9
  98.0 66.7 all-gather.11
  166.6 66.7 all-gather.13
  235.1 66.7 all-gather.15
  303.7 66.7 all-gather.17
  372.2 66.7 all-gather.19
  440.8 66.7 all-gather.21
  509.5 66.7 all-gather.23
  753.8 92.8 all-reduce.2
